TPU v7x, 512 devices: a whole 4x4x16 slice. The times are simulated.
512 devices in a mesh: dp: 64 (over z, y_lo, core), expert: 8 (over y_hi, x).
Axes of the slice: x: 4, y: 4 (y_hi: 2, y_lo: 2; y = y_hi * 2 + y_lo), z: 16, core: 2. Of those that a mesh axis runs over, the one named last changes fastest.
Arguments:
- inputs: bfloat16 [256, 3072], P('dp', 'expert'), may hold values from -6 to 6
- routes: int32 [256, 2], P('dp'), may hold values from 0 to 7, all different within a row; in each aligned block of 4 rows (0 to 3, 4 to 7, ...) at most 2 rows name the same one
- combine: float32 [256, 2], P('dp'), may hold values from 0.1 to 1
- cotangent: bfloat16 [256, 3072], P('dp', 'expert'), may hold values from -6 to 6
- w_gate: bfloat16 [8, 3072, 8192], P('expert', None, 'dp'), may hold values from -0.109375 to 0.109375
- w_up: bfloat16 [8, 3072, 8192], P('expert', None, 'dp'), may hold values from -0.109375 to 0.109375
- w_down: bfloat16 [8, 8192, 3072], P('expert', 'dp'), may hold values from -0.0625 to 0.0625
Outputs:
- input_grad: bfloat16 [256, 3072], P('dp', 'expert')
- gate_grad: bfloat16 [8, 3072, 8192], P('expert', None, 'dp')
- up_grad: bfloat16 [8, 3072, 8192], P('expert', None, 'dp')
- down_grad: bfloat16 [8, 8192, 3072], P('expert', 'dp')
Inputs may be any that keep to these rules, and one draw needn't show every extreme that they name: `routes`: each token names two different experts. Among the tokens of one index of dp no expert is named more than 2 times, a bound that some block reaches there.
All inputs are finite; a program needn't handle non-finite values.
Results may differ from a plain program's by a relative error of at most 0.0065.
Values may be sent and summed in bfloat16 or wider, within the bound.
No kernel may reach another device: no remote copies, remote signals or barrier semaphores. Data moves between devices by JAX's collectives and lax.ppermute only.
A program may use at most 64 MiB of HBM per device.

v0:
```python
import jax
import jax.numpy as jnp
from jax import lax
from jax.sharding import PartitionSpec as P

MOST = 2


def forward_part(all_inputs, w_gate, w_up):
    gate_pre = jnp.einsum("rld,ldf->rlf", all_inputs, w_gate, preferred_element_type=jnp.float32)
    up_pre = jnp.einsum("rld,ldf->rlf", all_inputs, w_up, preferred_element_type=jnp.float32)
    gate_sig = jax.nn.sigmoid(gate_pre)
    activated = gate_pre * gate_sig
    hidden = (activated * up_pre).astype(jnp.bfloat16)
    return (gate_pre, up_pre, gate_sig, activated, hidden)


def per_device(inputs, routes, combine, cotangent, w_gate, w_up, w_down):
    local_experts = w_gate.shape[0]
    expert_count = local_experts * lax.axis_size("expert")
    slot_count = MOST
    width_part = inputs.shape[1]
    routes_flat = routes.reshape(-1)
    onehot = (routes_flat[:, None] == jnp.arange(expert_count, dtype=jnp.int32)[None, :]).astype(
        jnp.int32
    )
    before = jnp.cumsum(onehot, axis=0) - onehot
    slot_index = jnp.sum(before * onehot, axis=1)
    column = slot_index * expert_count + routes_flat
    placer = column[:, None] == jnp.arange(slot_count * expert_count, dtype=jnp.int32)[None, :]
    placer_half = placer.astype(jnp.bfloat16)
    repeated = jnp.repeat(inputs, 2, axis=0)
    scaled = (
        combine.reshape(-1)[:, None] * jnp.repeat(cotangent, 2, axis=0).astype(jnp.float32)
    ).astype(jnp.bfloat16)
    sent_inputs = jnp.einsum(
        "jc,jd->cd", placer_half, repeated, preferred_element_type=jnp.float32
    ).astype(jnp.bfloat16)
    sent_grads = jnp.einsum(
        "jc,jd->cd", placer_half, scaled, preferred_element_type=jnp.float32
    ).astype(jnp.bfloat16)
    sent_inputs = sent_inputs.reshape(slot_count, expert_count, width_part)
    sent_grads = sent_grads.reshape(slot_count, expert_count, width_part)
    expert_inputs, expert_grads = (
        lax.all_to_all(sent_inputs, "expert", split_axis=1, concat_axis=2, tiled=True),
        lax.all_to_all(sent_grads, "expert", split_axis=1, concat_axis=2, tiled=True),
    )
    all_inputs, all_grads = (
        lax.all_gather(expert_inputs, "dp", axis=0, tiled=True),
        lax.all_gather(expert_grads, "dp", axis=0, tiled=True),
    )
    gate_pre, up_pre, gate_sig, activated, hidden = forward_part(all_inputs, w_gate, w_up)
    hidden_delta = jnp.einsum("rld,lfd->rlf", all_grads, w_down, preferred_element_type=jnp.float32)
    down_grad = jnp.einsum(
        "rlf,rld->lfd", hidden, all_grads, preferred_element_type=jnp.float32
    ).astype(jnp.bfloat16)
    gate_delta = (hidden_delta * up_pre * gate_sig * (1.0 + gate_pre * (1.0 - gate_sig))).astype(
        jnp.bfloat16
    )
    up_delta = (hidden_delta * activated).astype(jnp.bfloat16)
    gate_grad = jnp.einsum(
        "rld,rlf->ldf", all_inputs, gate_delta, preferred_element_type=jnp.float32
    ).astype(jnp.bfloat16)
    up_grad = jnp.einsum(
        "rld,rlf->ldf", all_inputs, up_delta, preferred_element_type=jnp.float32
    ).astype(jnp.bfloat16)
    from_gate = jnp.einsum("rlf,ldf->rld", gate_delta, w_gate, preferred_element_type=jnp.float32)
    from_up = jnp.einsum("rlf,ldf->rld", up_delta, w_up, preferred_element_type=jnp.float32)
    own_rows = lax.psum_scatter(from_gate + from_up, "dp", scatter_dimension=0, tiled=True)
    back_rows = lax.all_to_all(own_rows, "expert", split_axis=2, concat_axis=1, tiled=True)
    back_flat = back_rows.reshape(slot_count * expert_count, width_part)
    assign_grad = jnp.dot(placer.astype(jnp.float32), back_flat, precision=lax.Precision.HIGHEST)
    input_grad = jnp.sum(assign_grad.reshape(inputs.shape[0], 2, width_part), axis=1).astype(
        jnp.bfloat16
    )
    return (input_grad, gate_grad, up_grad, down_grad)


def solution(mesh):
    placed = (
        P("dp", "expert"),
        P("dp", None),
        P("dp", None),
        P("dp", "expert"),
        P("expert", None, "dp"),
        P("expert", None, "dp"),
        P("expert", "dp", None),
    )
    return jax.shard_map(
        per_device,
        mesh=mesh,
        in_specs=placed,
        out_specs=(
            P("dp", "expert"),
            P("expert", None, "dp"),
            P("expert", None, "dp"),
            P("expert", "dp", None),
        ),
        check_vma=False,
    )
```

profile of v0, /device:TPU:1, one launch (start us, length us, event | category | flops | bytes accessed | tf_op | source)
XLA Modules:
  0.0 658.0 jit_solution(9490560236936488608)
XLA Ops:
  7.2 0.0 copy-start
  7.2 0.8 copy.37
  8.0 0.1 eq.50
  8.1 0.1 fusion.28
  8.2 0.2 select_reduce_fusion
  8.4 0.7 broadcast_in_dim.10
  9.1 0.3 fusion.5
  9.4 0.6 copy.43
  10.0 7.5 %all-to-all-start.1 = ((bf16[2,8,384]{2,0,1:T(2,128)(2,1)}), bf16[2,8,384]{2,0,1:T(2,128)(2,1)S(1)}, u32[]{:S(2)}, u32[]{:S(2)}) async-start(bf16[2,8,384]{2,0,1:T(2,128)(2,1)} %copy.43), calls=%async_computation.1 | async-start | bytes 24576 | tf_op jit(solution)/shard_map/all_to_all | solution.py:45
  17.5 0.8 copy.40
  18.2 0.1 mul.48
  18.3 0.7 broadcast_in_dim.4
  19.0 0.3 fusion.4
  19.3 0.6 copy.41
  19.9 4.1 all-to-all-done.1
  24.0 3.3 all-to-all-start
  27.4 0.0 all-reduce.3.cloned.1.call-start
  27.4 6.4 all-to-all-done
  33.9 76.2 %all_gather.6 = bf16[128,1,3072]{2,1,0:T(2,128)(2,1)S(1)} all-gather(bf16[2,1,3072]{2,1,0:T(2,128)(2,1)S(1)} %copy.42), channel_id=1, replica_groups=mesh['dp'=64,'expert'=8] {'dp'}, dimensions={0}, use_global_device_ids=true | all-gather | bytes 798720 | tf_op jit(solution)/shard_map/all_gather | solution.py:50
  110.1 63.8 %all_gather.7 = bf16[128,1,3072]{2,1,0:T(2,128)(2,1)S(1)} all-gather(bf16[2,1,3072]{2,1,0:T(2,128)(2,1)S(1)} %copy.44), channel_id=1, replica_groups=mesh['dp'=64,'expert'=8] {'dp'}, dimensions={0}, use_global_device_ids=true | all-gather | bytes 798720 | tf_op jit(solution)/shard_map/all_gather | solution.py:49
  173.8 0.0 copy-start.1
  173.8 0.2 copy.50
  174.1 0.0 copy-done
  174.1 0.0 copy-start.2
  174.1 0.4 convolution_bitcast_fusion
  174.5 0.5 copy-done.1
  175.0 0.4 convolution_bitcast_fusion.1
  175.3 0.0 copy-done.2
  175.3 0.4 fusion.21
  175.8 0.4 fusion.12
  176.1 1.5 fusion
  177.6 0.0 all-reduce.3.cloned.1.call-update
  177.7 0.1 mul.47
  177.8 0.1 copy.39
  177.9 1.3 dynamic-slice
  179.8 1.3 fusion.2
  181.1 1.3 fusion.3
  182.4 429.8 %all-reduce.3.cloned.1.call-done = f32[128,1,3072]{2,0,1:T(8,128)} async-done(((f32[128,1,3072]{2,0,1:T(8,128)}), f32[128,1,3072]{2,0,1:T(8,128)}) %all-reduce.3.cloned.1.call-update) | async-done | bytes 1572880
  612.2 0.9 constant_dynamic-slice_fusion
  613.1 1.6 copy.45
  614.7 0.5 broadcast.50
  615.2 14.8 %reduce = f32[3072,2]{1,0:T(8,128)} reduce(f32[3072,1,2]{2,1,0:T(1,128)S(1)} %bitcast.92, f32[]{:T(128)} %broadcast.50), dimensions={1}, to_apply=%bitcast.79.reduce_sub_computation | reduce | bytes 49156
  630.0 3.0 reshape.131
  633.1 6.2 all-to-all-start.2
  639.2 1.3 fusion.1
  640.5 5.3 all-to-all-done.2
  645.8 0.7 reduce.1
  646.5 2.5 reshape.132
  649.1 1.3 copy.46
  650.4 0.8 convolution_reduce_fusion
  (8 shorter events, 0.1 us)
Async XLA Ops:
  7.2 166.9 %copy-start = (bf16[1,3072,128]{2,1,0:T(8,128)(2,1)S(1)}, bf16[1,3072,128]{2,1,0:T(8,128)(2,1)}, u32[]{:S(2)}) copy-start(bf16[1,3072,128]{2,1,0:T(8,128)(2,1)} %param.11) | copy-start | bytes 2359300
  10.0 14.0 %all-to-all-start.1 = ((bf16[2,8,384]{2,0,1:T(2,128)(2,1)}), bf16[2,8,384]{2,0,1:T(2,128)(2,1)S(1)}, u32[]{:S(2)}, u32[]{:S(2)}) async-start(bf16[2,8,384]{2,0,1:T(2,128)(2,1)} %copy.43), calls=%async_computation.1 | async-start | bytes 24576 | tf_op jit(solution)/shard_map/all_to_all | solution.py:45
  24.0 9.8 %all-to-all-start = ((bf16[2,8,384]{2,0,1:T(2,128)(2,1)}), bf16[2,8,384]{2,0,1:T(2,128)(2,1)S(1)}, u32[]{:S(2)}, u32[]{:S(2)}) async-start(bf16[2,8,384]{2,0,1:T(2,128)(2,1)} %copy.41), calls=%async_computation | async-start | bytes 24576 | tf_op jit(solution)/shard_map/all_to_all | solution.py:46
  27.4 584.8 %all-reduce.3.cloned.1.call-start = ((), (), s32[]{:S(2)}) async-start(), calls=%async_computation.3 | async-start | bytes 3145728
  173.8 1.1 copy-start.1
  174.1 1.2 copy-start.2
  633.1 12.7 %all-to-all-start.2 = ((f32[8,1,768]{2,1,0:T(1,128)}), f32[8,1,768]{2,1,0:T(1,128)S(1)}, u32[]{:S(2)}, u32[]{:S(2)}) async-start(f32[8,1,768]{2,1,0:T(1,128)} %reshape.131), calls=%async_computation.2 | async-start | bytes 49152 | tf_op jit(solution)/shard_map/all_to_all | solution.py:70
Sparse Core Ops, SparseCore 0:
  177.8 434.3 all-reduce.2
where the time goes:
time: 659 us; the launch traced here: 658 us
  waiting for transfers between devices  446 us (68%)
  blocking collectives  140 us (21%)
  starting transfers between devices  17 us (3%)
  local copies, waits for them, and re-layouts  16.5 us (3%)
  other arithmetic  15.8 us (2%)
  between operations  14.8 us (2%)
  matrix products  8.23 us (1%)
    unnamed x2, waiting for transfers between devices  430 us
    all_gather x1, blocking collectives, per_device(): lax.all_gather(expert_grads, 'dp', axis=0, tiled=True)  76.2 us
    all_gather x1, blocking collectives, per_device(): lax.all_gather(expert_inputs, 'dp', axis=0, tiled=True)  63.8 us
    unnamed x1, other arithmetic  14.8 us
  transfers between devices with their start and end apart: 4, of which 4 were waited for; matrix products, arithmetic and copies ran while one was open for 1% of the time, Pallas kernels for 0%

commit v1 on v0

--- a/solution.py
+++ b/solution.py
@@ -67,7 +67,10 @@
     from_gate = jnp.einsum("rlf,ldf->rld", gate_delta, w_gate, preferred_element_type=jnp.float32)
     from_up = jnp.einsum("rlf,ldf->rld", up_delta, w_up, preferred_element_type=jnp.float32)
     own_rows = lax.psum_scatter(from_gate + from_up, "dp", scatter_dimension=0, tiled=True)
-    back_rows = lax.all_to_all(own_rows, "expert", split_axis=2, concat_axis=1, tiled=True)
+    count = lax.axis_size("expert")
+    blocks = jnp.stack(jnp.split(own_rows, count, axis=2), axis=0)
+    blocks = lax.all_to_all(blocks, "expert", split_axis=0, concat_axis=0)
+    back_rows = jnp.concatenate(blocks, axis=1)
     back_flat = back_rows.reshape(slot_count * expert_count, width_part)
     assign_grad = jnp.dot(placer.astype(jnp.float32), back_flat, precision=lax.Precision.HIGHEST)
     input_grad = jnp.sum(assign_grad.reshape(inputs.shape[0], 2, width_part), axis=1).astype(

time: 659 us -> 645 us (0.979)
  other arithmetic: 15.8 us -> 0.3 us
    unnamed x1 -> x0, other arithmetic: 14.8 us -> none
    unnamed x14 -> x17, local copies, waits for them, and re-layouts: 10.6 us -> 13.2 us
where the time goes in v1:
time: 645 us; the launch traced here: 644 us
  waiting for transfers between devices  446 us (69%)
  blocking collectives  140 us (22%)
  local copies, waits for them, and re-layouts  17.6 us (3%)
  starting transfers between devices  17 us (3%)
  between operations  14.8 us (2%)
  matrix products  8.24 us (1%)
    unnamed x2, waiting for transfers between devices  430 us
    all_gather x1, blocking collectives, per_device(): lax.all_gather(expert_grads, 'dp', axis=0, tiled=True)  76.2 us
    all_gather x1, blocking collectives, per_device(): lax.all_gather(expert_inputs, 'dp', axis=0, tiled=True)  63.8 us
    unnamed x17, local copies, waits for them, and re-layouts  13.2 us
  transfers between devices with their start and end apart: 4, of which 4 were waited for; matrix products, arithmetic and copies ran while one was open for 1% of the time, Pallas kernels for 0%

profile of v1, /device:TPU:1, one launch (start us, length us, event | category | flops | bytes accessed | tf_op | source)
XLA Modules:
  0.0 643.5 jit_solution(12326835436212964745)
XLA Ops:
  7.2 0.0 copy-start
  7.2 0.8 copy.59
  8.0 0.1 eq.50
  8.1 0.1 fusion.30
  8.2 0.2 select_reduce_fusion
  8.4 0.7 broadcast_in_dim.10
  9.1 0.3 fusion.5
  9.4 0.6 copy.65
  10.0 7.5 %all-to-all-start.1 = ((bf16[2,8,384]{2,0,1:T(2,128)(2,1)}), bf16[2,8,384]{2,0,1:T(2,128)(2,1)S(1)}, u32[]{:S(2)}, u32[]{:S(2)}) async-start(bf16[2,8,384]{2,0,1:T(2,128)(2,1)} %copy.65), calls=%async_computation.1 | async-start | bytes 24576 | tf_op jit(solution)/shard_map/all_to_all | solution.py:45
  17.5 0.8 copy.62
  18.2 0.1 mul.48
  18.3 0.7 broadcast_in_dim.4
  19.0 0.3 fusion.4
  19.3 0.6 copy.63
  19.9 4.1 all-to-all-done.1
  24.0 3.3 all-to-all-start
  27.4 0.0 all-reduce.3.cloned.1.call-start
  27.4 6.4 all-to-all-done
  33.9 76.2 %all_gather.6 = bf16[128,1,3072]{2,1,0:T(2,128)(2,1)S(1)} all-gather(bf16[2,1,3072]{2,1,0:T(2,128)(2,1)S(1)} %copy.64), channel_id=1, replica_groups=mesh['dp'=64,'expert'=8] {'dp'}, dimensions={0}, use_global_device_ids=true | all-gather | bytes 798720 | tf_op jit(solution)/shard_map/all_gather | solution.py:50
  110.1 63.8 %all_gather.7 = bf16[128,1,3072]{2,1,0:T(2,128)(2,1)S(1)} all-gather(bf16[2,1,3072]{2,1,0:T(2,128)(2,1)S(1)} %copy.66), channel_id=1, replica_groups=mesh['dp'=64,'expert'=8] {'dp'}, dimensions={0}, use_global_device_ids=true | all-gather | bytes 798720 | tf_op jit(solution)/shard_map/all_gather | solution.py:49
  173.8 0.0 copy-start.1
  173.8 0.2 copy.71
  174.1 0.0 copy-done
  174.1 0.0 copy-start.2
  174.1 0.4 convolution_bitcast_fusion
  174.5 0.5 copy-done.1
  175.0 0.4 convolution_bitcast_fusion.1
  175.3 0.0 copy-done.2
  175.3 0.4 fusion.21
  175.8 0.4 fusion.12
  176.1 1.5 fusion
  177.7 0.0 all-reduce.3.cloned.1.call-update
  177.7 0.1 mul.47
  177.8 0.1 copy.61
  177.9 1.3 dynamic-slice
  179.8 1.3 fusion.2
  181.1 1.3 fusion.3
  182.4 429.8 %all-reduce.3.cloned.1.call-done = f32[128,1,3072]{2,0,1:T(8,128)} async-done(((f32[128,1,3072]{2,0,1:T(8,128)}), f32[128,1,3072]{2,0,1:T(8,128)}) %all-reduce.3.cloned.1.call-update) | async-done | bytes 1572880
  612.2 1.3 constant_dynamic-update-slice_fusion.7
  613.5 1.4 constant_dynamic-update-slice_fusion.6
  614.9 1.4 constant_dynamic-update-slice_fusion.5
  616.3 1.4 constant_dynamic-update-slice_fusion.4
  617.6 1.4 constant_dynamic-update-slice_fusion.3
  619.0 1.4 constant_dynamic-update-slice_fusion.2
  620.4 1.4 constant_dynamic-update-slice_fusion.1
  621.8 1.4 constant_dynamic-update-slice_fusion
  623.1 6.1 all-to-all-start.2
  629.3 1.3 fusion.1
  630.6 5.3 all-to-all-done.2
  635.9 0.8 convolution_reduce_fusion
  (7 shorter events, 0.1 us)
Async XLA Ops:
  7.2 166.9 %copy-start = (bf16[1,3072,128]{2,1,0:T(8,128)(2,1)S(1)}, bf16[1,3072,128]{2,1,0:T(8,128)(2,1)}, u32[]{:S(2)}) copy-start(bf16[1,3072,128]{2,1,0:T(8,128)(2,1)} %param.11) | copy-start | bytes 2359300
  10.0 14.0 %all-to-all-start.1 = ((bf16[2,8,384]{2,0,1:T(2,128)(2,1)}), bf16[2,8,384]{2,0,1:T(2,128)(2,1)S(1)}, u32[]{:S(2)}, u32[]{:S(2)}) async-start(bf16[2,8,384]{2,0,1:T(2,128)(2,1)} %copy.65), calls=%async_computation.1 | async-start | bytes 24576 | tf_op jit(solution)/shard_map/all_to_all | solution.py:45
  24.0 9.8 %all-to-all-start = ((bf16[2,8,384]{2,0,1:T(2,128)(2,1)}), bf16[2,8,384]{2,0,1:T(2,128)(2,1)S(1)}, u32[]{:S(2)}, u32[]{:S(2)}) async-start(bf16[2,8,384]{2,0,1:T(2,128)(2,1)} %copy.63), calls=%async_computation | async-start | bytes 24576 | tf_op jit(solution)/shard_map/all_to_all | solution.py:46
  27.4 584.8 %all-reduce.3.cloned.1.call-start = ((), (), s32[]{:S(2)}) async-start(), calls=%async_computation.3 | async-start | bytes 3145728
  173.8 1.1 copy-start.1
  174.1 1.2 copy-start.2
  623.1 12.7 %all-to-all-start.2 = ((f32[8,2,1,384]{3,1,2,0:T(2,128)}), f32[8,2,1,384]{3,1,2,0:T(2,128)S(1)}, u32[]{:S(2)}, u32[]{:S(2)}) async-start(f32[8,2,1,384]{3,1,2,0:T(2,128)} %constant_dynamic-update-slice_fusion), calls=%async_computation.2 | async-start | bytes 49152 | tf_op jit(solution)/shard_map/all_to_all | solution.py:72
Sparse Core Ops, SparseCore 0:
  177.8 434.3 all-reduce.2
